TPU v7x, 32 devices: a whole 2x2x4 slice. The times are simulated.
32 devices in a mesh: seq: 8 (over y, x, core), head: 4 (over z).
Axes of the slice: x: 2, y: 2, z: 4, core: 2. Of those that a mesh axis runs over, the one named last changes fastest.
Arguments:
- queries: bfloat16 [4096, 64, 128], P(('seq', 'head')), may hold values from -36 to 36
- keys: bfloat16 [4096, 8, 128], P(('seq', 'head')), may hold values from -6 to 6
- values: bfloat16 [4096, 8, 128], P(('seq', 'head')), may hold values from -6 to 6
- output_gradient: bfloat16 [4096, 64, 128], P(('seq', 'head')), may hold values from -6 to 6
- global_blocks: int32 [2], replicated, may hold values from 0 to 31, as said below
- random_blocks: int32 [32, 3], replicated, may hold values from 0 to 31, as said below
Outputs:
- out: bfloat16 [4096, 64, 128], P(('seq', 'head'))
- grad_queries: bfloat16 [4096, 64, 128], P(('seq', 'head'))
- grad_keys: bfloat16 [4096, 8, 128], P(('seq', 'head'))
- grad_values: bfloat16 [4096, 8, 128], P(('seq', 'head'))
Inputs may be any that keep to these rules, and one draw needn't show every extreme that they name: `global_blocks`: the two blocks differ; one of them is the last block, 31. `random_blocks`: call 4 consecutive blocks starting at a multiple of 4 a group. The entries listed by a group's query blocks never lie in that group's own blocks, and at most 2 of them lie in any one other group; in every group some other group is hit exactly 2 times.
All inputs are finite; a program needn't handle non-finite values.
Results may differ from a plain program's by a relative error of at most 0.035.
Values may be sent and summed in bfloat16 or wider, within the bound.
No kernel may reach another device: no remote copies, remote signals or barrier semaphores. Data moves between devices by JAX's collectives and lax.ppermute only.
A program may use at most 128 MiB of HBM per device.

v0:
```python
import math
import jax
import jax.numpy as jnp
from jax import lax
from jax.sharding import PartitionSpec as P

BLOCK_TOKENS = 128


def padded(shard, sides, width):
    for axis, dim in sides:
        count, length = (lax.axis_size(axis), shard.shape[dim])
        up = [(i, (i + 1) % count) for i in range(count - 1)]
        down = [(j, i) for i, j in up]
        last = lax.slice_in_dim(shard, length - width, length, axis=dim)
        leading = lax.slice_in_dim(shard, 0, width, axis=dim)
        before = lax.ppermute(last, axis, up)
        after = lax.ppermute(leading, axis, down)
        shard = jnp.concatenate([before, shard, after], axis=dim)
    return shard


def from_root(block, axis, owner):
    block = jnp.where(lax.axis_index(axis) == owner, block, jnp.zeros_like(block))
    return lax.psum(block, axis)


def per_device(queries, keys, values, output_gradient, global_blocks, random_blocks):
    query_loc, key_loc, value_loc, grad_loc = (
        lax.all_to_all(queries, "head", split_axis=1, concat_axis=0, tiled=True),
        lax.all_to_all(keys, "head", split_axis=1, concat_axis=0, tiled=True),
        lax.all_to_all(values, "head", split_axis=1, concat_axis=0, tiled=True),
        lax.all_to_all(output_gradient, "head", split_axis=1, concat_axis=0, tiled=True),
    )
    shard_len, heads_q, head_width = query_loc.shape
    heads_kv = key_loc.shape[1]
    heads_per_group = heads_q // heads_kv
    kv_width = heads_kv * head_width
    blocks = shard_len // BLOCK_TOKENS
    seq_count = lax.axis_size("seq")
    own_index = lax.axis_index("seq")
    block_total_count = seq_count * blocks
    capacity = (3 * blocks + seq_count - 2) // (seq_count - 1)
    entry_count = 3 * blocks
    score_scale = 1.0 / math.sqrt(head_width)
    kv_pair = jnp.stack(
        [key_loc.reshape(shard_len, kv_width), value_loc.reshape(shard_len, kv_width)]
    )
    extended = padded(kv_pair, (("seq", 1),), BLOCK_TOKENS)
    kv_tiles = kv_pair.reshape(2, blocks, BLOCK_TOKENS, kv_width).transpose(1, 0, 2, 3)
    global_owner = global_blocks // blocks
    global_offset = global_blocks % blocks
    own_global = (jnp.arange(blocks)[None, :] == global_offset[:, None]) & (
        global_owner == own_index
    )[:, None]
    received_rows = []
    for global_slot in range(2):
        candidate = lax.dynamic_index_in_dim(
            kv_tiles, global_offset[global_slot], 0, keepdims=False
        )
        received_rows.append(from_root(candidate, "seq", global_owner[global_slot]))
    global_tiles = jnp.stack(received_rows)
    all_entries = (
        random_blocks.reshape(seq_count, blocks, 3)
        .transpose(0, 2, 1)
        .reshape(seq_count, entry_count)
    )
    all_owner = all_entries // blocks
    entry_ids = jnp.arange(entry_count)
    entry_earlier = entry_ids[None, :] < entry_ids[:, None]
    all_rank = jnp.sum(
        (all_owner[:, :, None] == all_owner[:, None, :]) & entry_earlier[None], axis=2
    )
    my_entries = lax.dynamic_index_in_dim(all_entries, own_index, 0, keepdims=False)
    my_owner = lax.dynamic_index_in_dim(all_owner, own_index, 0, keepdims=False)
    my_rank = lax.dynamic_index_in_dim(all_rank, own_index, 0, keepdims=False)
    my_slot = my_owner * capacity + my_rank
    owned_here = (all_owner == own_index)[:, :, None] & (
        all_rank[:, :, None] == jnp.arange(capacity)[None, None, :]
    )
    offset_match = (all_entries % blocks)[:, :, None] == jnp.arange(blocks)[None, None, :]
    selector = jnp.einsum(
        "tec,teo->tco",
        owned_here.astype(jnp.bfloat16),
        offset_match.astype(jnp.bfloat16),
        preferred_element_type=jnp.float32,
    ).astype(jnp.bfloat16)
    everything = lax.all_gather(kv_pair, "seq", axis=1, tiled=True)
    tiled_all = everything.reshape(2, block_total_count, BLOCK_TOKENS, kv_width)
    random_tiles = jnp.take(tiled_all, my_entries, axis=1).transpose(1, 0, 2, 3)
    random_by_block = random_tiles.reshape(3, blocks, 2, BLOCK_TOKENS, kv_width).transpose(
        1, 0, 2, 3, 4
    )
    block_ids = own_index * blocks + jnp.arange(blocks)
    listed = jnp.concatenate(
        [
            jnp.stack([block_ids - 1, block_ids, block_ids + 1], axis=1),
            jnp.broadcast_to(global_blocks[None, :], (blocks, 2)),
            my_entries.reshape(3, blocks).T,
        ],
        axis=1,
    )
    inside = (listed >= 0) & (listed < block_total_count)
    tile_ids = jnp.arange(8)
    tile_earlier = tile_ids[None, :] < tile_ids[:, None]
    repeat = jnp.any((listed[:, :, None] == listed[:, None, :]) & tile_earlier[None], axis=2)
    live = inside & jnp.logical_not(repeat)

    def attend(unused_state, inputs):
        query_blk, grad_blk, random_blk, live_row, position = inputs
        near_tiles = lax.dynamic_slice_in_dim(
            extended, position * BLOCK_TOKENS, 3 * BLOCK_TOKENS, 1
        )
        near_tiles = near_tiles.reshape(2, 3, BLOCK_TOKENS, kv_width).transpose(1, 0, 2, 3)
        all_tiles = jnp.concatenate([near_tiles, global_tiles, random_blk], axis=0)
        key_t = all_tiles[:, 0].reshape(8, BLOCK_TOKENS, heads_kv, head_width)
        value_t = all_tiles[:, 1].reshape(8, BLOCK_TOKENS, heads_kv, head_width)
        query_grid = query_blk.reshape(BLOCK_TOKENS, heads_kv, heads_per_group, head_width)
        grad_grid = grad_blk.reshape(BLOCK_TOKENS, heads_kv, heads_per_group, head_width)
        scores = (
            jnp.einsum("qkgd,tbkd->kgqtb", query_grid, key_t, preferred_element_type=jnp.float32)
            * score_scale
        )
        scores = jnp.where(live_row[None, None, None, :, None], scores, -jnp.inf)
        row_max = jnp.max(scores, axis=(3, 4), keepdims=True)
        expo = jnp.exp(scores - row_max)
        attn_prob = expo / jnp.sum(expo, axis=(3, 4), keepdims=True)
        prob_low = attn_prob.astype(jnp.bfloat16)
        attended = jnp.einsum(
            "kgqtb,tbkd->qkgd", prob_low, value_t, preferred_element_type=jnp.float32
        )
        out_low = attended.astype(jnp.bfloat16)
        row_delta = jnp.sum(grad_grid.astype(jnp.float32) * out_low.astype(jnp.float32), axis=-1)
        grad_prob = jnp.einsum(
            "qkgd,tbkd->kgqtb", grad_grid, value_t, preferred_element_type=jnp.float32
        )
        grad_score = attn_prob * (
            grad_prob - jnp.transpose(row_delta, (1, 2, 0))[:, :, :, None, None]
        )
        score_low = grad_score.astype(jnp.bfloat16)
        query_grad = (
            jnp.einsum("kgqtb,tbkd->qkgd", score_low, key_t, preferred_element_type=jnp.float32)
            * score_scale
        )
        key_grad = (
            jnp.einsum(
                "kgqtb,qkgd->tbkd", score_low, query_grid, preferred_element_type=jnp.float32
            )
            * score_scale
        )
        value_grad = jnp.einsum(
            "kgqtb,qkgd->tbkd", prob_low, grad_grid, preferred_element_type=jnp.float32
        )
        tile_terms = jnp.stack(
            [
                key_grad.reshape(8, BLOCK_TOKENS, kv_width),
                value_grad.reshape(8, BLOCK_TOKENS, kv_width),
            ],
            axis=1,
        )
        return (
            unused_state,
            (
                out_low.reshape(BLOCK_TOKENS, heads_q, head_width),
                query_grad.astype(jnp.bfloat16).reshape(BLOCK_TOKENS, heads_q, head_width),
                tile_terms,
            ),
        )

    unused_final, (output_block_rows, query_gradient_rows, tile_grads) = lax.scan(
        attend,
        0,
        (
            query_loc.reshape(blocks, BLOCK_TOKENS, heads_q, head_width),
            grad_loc.reshape(blocks, BLOCK_TOKENS, heads_q, head_width),
            random_by_block,
            live,
            jnp.arange(blocks),
        ),
    )
    pad_spec_low = ((0, 2), (0, 0), (0, 0), (0, 0))
    pad_spec_mid = ((1, 1), (0, 0), (0, 0), (0, 0))
    pad_spec_high = ((2, 0), (0, 0), (0, 0), (0, 0))
    window_sum = (
        jnp.pad(tile_grads[:, 0], pad_spec_low)
        + jnp.pad(tile_grads[:, 1], pad_spec_mid)
        + jnp.pad(tile_grads[:, 2], pad_spec_high)
    )
    rims = jnp.concatenate([window_sum[0], window_sum[blocks + 1]], axis=1)
    returned_rims = padded(rims.astype(jnp.bfloat16), (("seq", 1),), BLOCK_TOKENS).astype(
        rims.dtype
    )
    interior = window_sum[1 : blocks + 1]
    interior = (
        interior.at[0]
        .add(returned_rims[:, :BLOCK_TOKENS])
        .at[blocks - 1]
        .add(returned_rims[:, 3 * BLOCK_TOKENS :])
    )
    global_terms = jnp.sum(tile_grads[:, 3:5], axis=0)
    global_total = lax.psum(global_terms.astype(jnp.bfloat16), "seq").astype(jnp.float32)
    own_weight = own_global.astype(jnp.float32)[:, :, None, None, None]
    interior = interior + jnp.sum(own_weight * global_total[:, None], axis=0)
    random_terms = (
        tile_grads[:, 5:8]
        .transpose(1, 0, 2, 3, 4)
        .reshape(entry_count, 2, BLOCK_TOKENS, kv_width)
        .astype(jnp.bfloat16)
    )
    slot_onehot = (my_slot[:, None] == jnp.arange(seq_count * capacity)[None, :]).astype(
        jnp.bfloat16
    )
    back_buffer = jnp.einsum(
        "es,exbw->sxbw", slot_onehot, random_terms, preferred_element_type=jnp.float32
    ).astype(jnp.bfloat16)
    returned_terms = lax.all_to_all(back_buffer, "seq", split_axis=0, concat_axis=0, tiled=True)
    interior = interior + jnp.einsum(
        "tco,tcxbw->oxbw",
        selector,
        returned_terms.reshape(seq_count, capacity, 2, BLOCK_TOKENS, kv_width),
        preferred_element_type=jnp.float32,
    )
    kv_grad = interior.transpose(1, 0, 2, 3).reshape(2, shard_len, kv_width).astype(jnp.bfloat16)
    out_all = output_block_rows.reshape(shard_len, heads_q, head_width)
    query_grad_all = query_gradient_rows.reshape(shard_len, heads_q, head_width)
    key_grad_all = kv_grad[0].reshape(shard_len, heads_kv, head_width)
    value_grad_all = kv_grad[1].reshape(shard_len, heads_kv, head_width)
    return (
        lax.all_to_all(out_all, "head", split_axis=0, concat_axis=1, tiled=True),
        lax.all_to_all(query_grad_all, "head", split_axis=0, concat_axis=1, tiled=True),
        lax.all_to_all(key_grad_all, "head", split_axis=0, concat_axis=1, tiled=True),
        lax.all_to_all(value_grad_all, "head", split_axis=0, concat_axis=1, tiled=True),
    )


def solution(mesh):
    placed = (
        P(("seq", "head"), None, None),
        P(("seq", "head"), None, None),
        P(("seq", "head"), None, None),
        P(("seq", "head"), None, None),
        P(),
        P(),
    )
    return jax.shard_map(
        per_device,
        mesh=mesh,
        in_specs=placed,
        out_specs=(
            P(("seq", "head"), None, None),
            P(("seq", "head"), None, None),
            P(("seq", "head"), None, None),
            P(("seq", "head"), None, None),
        ),
        check_vma=False,
    )
```

profile of v0, /device:TPU:0, one launch (start us, length us, event | category | flops | bytes accessed | tf_op | source)
XLA Modules:
  0.0 494.7 jit_solution(17608688807124787782)
XLA Ops:
  8.9 6.3 %all-to-all-start = ((bf16[128,8,128]{2,0,1:T(8,128)(2,1)}), bf16[128,8,128]{2,0,1:T(8,128)(2,1)S(1)}, u32[]{:S(2)}, u32[]{:S(2)}) async-start(bf16[128,8,128]{2,0,1:T(8,128)(2,1)} %copy.314), calls=%async_computation | async-start | bytes 524288 | tf_op jit(solution)/shard_map/all_to_all | solution.py:31
  16.9 7.2 %all-to-all-done = bf16[128,8,128]{2,0,1:T(8,128)(2,1)S(1)} async-done(((bf16[128,8,128]{2,0,1:T(8,128)(2,1)}), bf16[128,8,128]{2,0,1:T(8,128)(2,1)S(1)}, u32[]{:S(2)}, u32[]{:S(2)}) %all-to-all-start) | async-done | bytes 262176 | tf_op jit(solution)/shard_map/all_to_all | solution.py:31
  24.1 3.4 all-to-all-start.1
  28.1 6.5 %all-to-all-done.1 = bf16[128,8,128]{2,0,1:T(8,128)(2,1)S(1)} async-done(((bf16[128,8,128]{2,0,1:T(8,128)(2,1)}), bf16[128,8,128]{2,0,1:T(8,128)(2,1)S(1)}, u32[]{:S(2)}, u32[]{:S(2)}) %all-to-all-start.1) | async-done | bytes 262176 | tf_op jit(solution)/shard_map/all_to_all | solution.py:32
  35.8 2.7 copy.323
  38.5 3.7 all-to-all-start.3
  45.5 4.3 copy.322
  50.4 37.3 %all-to-all-done.3 = bf16[128,64,128]{2,0,1:T(8,128)(2,1)S(1)} async-done(((bf16[128,64,128]{2,0,1:T(8,128)(2,1)}), bf16[128,64,128]{2,0,1:T(8,128)(2,1)S(1)}, u32[]{:S(2)}, u32[]{:S(2)}) %all-to-all-start.3) | async-done | bytes 2097184 | tf_op jit(solution)/shard_map/all_to_all | solution.py:33
  87.7 4.5 all-to-all-start.2
  103.0 2.9 collective-permute-done.1
  106.8 2.7 copy.324
  109.4 2.8 gather_fusion
  113.7 47.8 %all-reduce.9.cloned.1.call-done = (bf16[1,2,128,256]{3,2,1,0:T(8,128)(2,1)}, bf16[1,2,128,256]{3,2,0,1:T(8,128)(2,1)}) async-done(((bf16[1,2,128,256]{3,2,1,0:T(8,128)(2,1)}, bf16[1,2,128,256]{3,2,0,1:T(8,128)(2,1)}), (bf16[1,2,128,256]{3,2,1,0:T(8,128)(2,1)}, bf16[1,2,128,256]{3,2,0,1:T(8,128)(2,1)})) %all-reduce.9.cloned.1.call-update) | async-done | bytes 262160 | tf_op jit(solution)/shard_map/psum | solution.py:25
  161.4 105.5 %while.16 = (s32[]{:T(128)}, bf16[4,128,16,128]{3,2,1,0:T(8,128)(2,1)}, bf16[4,128,16,128]{3,2,1,0:T(8,128)(2,1)}, f32[4,8,2,128,256]{3,4,1,2,0:T(8,128)}, s32[4...) while((s32[]{:T(128)}, ...), condition=%wide.region_7.8_spmd, body=%wide.region_3.7_spmd.sunk | while | flops 3265259520 | bytes 89202968 | solution.py:170
  168.7 1.9 bitcast_reduce_fusion.2
  172.3 2.2 fusion.114
  177.6 3.2 fusion.115
  195.1 1.9 bitcast_reduce_fusion.2
  198.7 2.2 fusion.114
  204.0 3.2 fusion.115
  221.4 1.9 bitcast_reduce_fusion.2
  223.3 1.7 fusion.113
  225.0 2.2 fusion.114
  230.3 3.2 fusion.115
  247.8 1.9 bitcast_reduce_fusion.2
  249.7 1.7 fusion.113
  251.4 2.2 fusion.114
  256.7 3.2 fusion.115
  266.9 9.1 %copy.331 = f32[4,8,2,128,256]{4,3,2,0,1:T(8,128)} copy(f32[4,8,2,128,256]{3,4,1,2,0:T(8,128)} %get-tuple-element.94) | data formatting | bytes 16777216 | tf_op jit(solution)/shard_map/while | solution.py:170
  276.1 2.1 slice.167
  279.2 2.1 copy.347
  281.3 3.6 all-to-all-start.6
  285.2 2.2 slice_bitcast_fusion.2
  288.9 2.3 collective-permute-start.2
  292.5 2.5 slice_reduce_fusion
  298.7 3.8 scatter-add.9
  302.5 50.8 %all-reduce.7.cloned.1.call-done = bf16[2,2,128,256]{2,3,0,1:T(8,128)(2,1)} async-done(((bf16[2,2,128,256]{2,3,0,1:T(8,128)(2,1)}), bf16[2,2,128,256]{2,3,0,1:T(8,128)(2,1)}) %all-reduce.7.cloned.1.call-update) | async-done | bytes 262160 | tf_op jit(solution)/shard_map/psum | solution.py:201
  353.3 1.9 copy.336
  355.2 2.4 multiply_reduce_fusion.1
  357.6 3.1 fusion.50
  361.7 4.6 all-to-all-start.8
  366.4 8.1 %all-to-all-done.8 = bf16[512,2,128]{2,1,0:T(2,128)(2,1)S(1)} async-done(((bf16[512,2,128]{2,1,0:T(2,128)(2,1)}), bf16[512,2,128]{2,1,0:T(2,128)(2,1)S(1)}, u32[]{:S(2)}, u32[]{:S(2)}) %all-to-all-start.8) | async-done | bytes 262176 | tf_op jit(solution)/shard_map/all_to_all | solution.py:232
  374.5 10.4 %all_to_all.137 = bf16[512,2,128]{2,1,0:T(2,128)(2,1)S(1)} all-to-all(bf16[512,2,128]{2,1,0:T(2,128)(2,1)S(1)} %reshape_squeeze.6), channel_id=1, replica_groups=mesh['seq'=8,'head'=4] {'head'}, dimensions={0} | all-to-all | bytes 524288 | tf_op jit(solution)/shard_map/all_to_all | solution.py:231
  384.9 50.3 %all_to_all.138 = bf16[512,16,128]{2,1,0:T(8,128)(2,1)} all-to-all(bf16[512,16,128]{2,1,0:T(8,128)(2,1)S(1)} %bitcast.276), channel_id=1, replica_groups=mesh['seq'=8,'head'=4] {'head'}, dimensions={0} | all-to-all | bytes 4194304 | tf_op jit(solution)/shard_map/all_to_all | solution.py:230
  435.3 3.6 all-to-all-start.4
  440.8 2.0 copy.330
  442.8 43.4 %all-to-all-done.4 = bf16[512,16,128]{2,1,0:T(8,128)(2,1)S(1)} async-done(((bf16[512,16,128]{2,1,0:T(8,128)(2,1)}), bf16[512,16,128]{2,1,0:T(8,128)(2,1)S(1)}, u32[]{:S(2)}, u32[]{:S(2)}) %all-to-all-start.4) | async-done | bytes 2097184 | tf_op jit(solution)/shard_map/all_to_all | solution.py:229
  486.1 2.0 copy.328
  (201 shorter events, 97.2 us)
Async XLA Ops:
  8.9 15.3 %all-to-all-start = ((bf16[128,8,128]{2,0,1:T(8,128)(2,1)}), bf16[128,8,128]{2,0,1:T(8,128)(2,1)S(1)}, u32[]{:S(2)}, u32[]{:S(2)}) async-start(bf16[128,8,128]{2,0,1:T(8,128)(2,1)} %copy.314), calls=%async_computation | async-start | bytes 524288 | tf_op jit(solution)/shard_map/all_to_all | solution.py:31
  16.9 18.9 %copy-start.3 = (bf16[128,64,128]{2,1,0:T(8,128)(2,1)S(1)}, bf16[128,64,128]{2,1,0:T(8,128)(2,1)}, u32[]{:S(2)}) copy-start(bf16[128,64,128]{2,1,0:T(8,128)(2,1)} %param.15) | copy-start | bytes 6291460
  24.1 10.4 %all-to-all-start.1 = ((bf16[128,8,128]{2,0,1:T(8,128)(2,1)}), bf16[128,8,128]{2,0,1:T(8,128)(2,1)S(1)}, u32[]{:S(2)}, u32[]{:S(2)}) async-start(bf16[128,8,128]{2,0,1:T(8,128)(2,1)} %copy.316), calls=%async_computation.1 | async-start | bytes 524288 | tf_op jit(solution)/shard_map/all_to_all | solution.py:32
  27.5 81.9 %all-gather.2.cloned.1.call-start = ((), (), s32[]{:S(2)}) async-start(), calls=%async_computation.9 | async-start | bytes 4718592 | tf_op jit(solution)/shard_map/all_gather | solution.py:88
  35.0 0.8 copy-start.1
  38.5 3.8 copy-start.14
  38.5 49.2 %all-to-all-start.3 = ((bf16[128,64,128]{2,0,1:T(8,128)(2,1)}), bf16[128,64,128]{2,0,1:T(8,128)(2,1)S(1)}, u32[]{:S(2)}, u32[]{:S(2)}) async-start(bf16[128,64,128]{2,0,1:T(8,128)(2,1)} %copy.323), calls=%async_computation.3 | async-start | bytes 4194304 | tf_op jit(solution)/shard_map/all_to_all | solution.py:33
  42.3 7.5 %copy-start.9 = (s32[2]{0:T(128)}, s32[2]{0:T(128)S(1)}, u32[]{:S(2)}) copy-start(s32[2]{0:T(128)S(1)} %and_select_fusion) | copy-start | bytes 28
  50.4 43.6 %copy-start.13 = (s32[32,3]{0,1:T(4,128)S(1)}, s32[32,3]{0,1:T(4,128)}, u32[]{:S(2)}) copy-start(s32[32,3]{0,1:T(4,128)} %param.17) | copy-start | bytes 1156
  50.4 48.5 %copy-start.2 = (bf16[2,512,256]{2,1,0:T(8,128)(2,1)S(1)}, bf16[2,512,256]{2,1,0:T(8,128)(2,1)}, u32[]{:S(2)}) copy-start(bf16[2,512,256]{2,1,0:T(8,128)(2,1)} %copy-done.1) | copy-start | bytes 1572868
  87.7 73.8 %all-to-all-start.2 = ((bf16[128,64,128]{2,0,1:T(8,128)(2,1)}), bf16[128,64,128]{2,0,1:T(8,128)(2,1)}, u32[]{:S(2)}, u32[]{:S(2)}) async-start(bf16[128,64,128]{2,0,1:T(8,128)(2,1)} %copy.322), calls=%async_computation.2 | async-start | bytes 4194304 | tf_op jit(solution)/shard_map/all_to_all | solution.py:30
  92.2 69.3 %all-reduce.9.cloned.1.call-start = ((), (), s32[]{:S(2)}) async-start(), calls=%async_computation.11 | async-start | bytes 524288 | tf_op jit(solution)/shard_map/psum | solution.py:25
  95.7 2.2 copy-start.7
  99.6 3.4 collective-permute-start
  100.8 5.0 %collective-permute-start.1 = (bf16[2,128,256]{2,1,0:T(8,128)(2,1)S(1)}, bf16[2,128,256]{2,1,0:T(8,128)(2,1)S(1)}, u32[]{:S(2)}, u32[]{:S(2)}) collective-permute-start(bf16[2,128,256]{2,1,0:T(8,128)(2,1)S(1)} %get-tuple-element.249), channel_id=1, source_target_pairs={{4,0},{8,4},{12,8},{16,12},{20,16},{24,20},{28,24},{5,1},{9,5},{13... | collective-permute-start | bytes 393224 | tf_op jit(solution)/shard_map/ppermute | solution.py:18
  276.1 2.1 copy-start.12
  281.3 3.7 copy-start.10
  281.3 3.7 copy-start.15
  281.3 3.8 copy-start.8
  281.3 3.8 copy-start.11
  281.3 3.8 copy-start.16
  281.3 76.3 %all-to-all-start.6 = ((bf16[16,2,128,256]{3,2,1,0:T(8,128)(2,1)}), bf16[16,2,128,256]{3,2,1,0:T(8,128)(2,1)S(1)}, u32[]{:S(2)}, u32[]{:S(2)}) async-start(bf16[16,2,128,256]{3,2,1,0:T(8,128)(2,1)} %copy.347), calls=%async_computation.6 | async-start | bytes 4194304 | tf_op jit(solution)/shard_map/all_to_all | solution.py:216
  284.9 68.4 %all-reduce.7.cloned.1.call-start = ((), (), s32[]{:S(2)}) async-start(), calls=%async_computation.10 | async-start | bytes 524288 | tf_op jit(solution)/shard_map/psum | solution.py:201
  288.9 7.4 %collective-permute-start.2 = (bf16[2,128,256]{2,1,0:T(8,128)(2,1)S(1)}, bf16[2,128,256]{2,1,0:T(8,128)(2,1)S(1)}, u32[]{:S(2)}, u32[]{:S(2)}) collective-permute-start(bf16[2,128,256]{2,1,0:T(8,128)(2,1)S(1)} %get-tuple-element.242), channel_id=1, source_target_pairs={{0,4},{4,8},{8,12},{12,16},{16,20},{20,24},{24,28},{1,5},{5,9},{9,... | collective-permute-start | bytes 393224 | tf_op jit(solution)/shard_map/ppermute | solution.py:17
  291.2 5.2 %collective-permute-start.3 = (bf16[2,128,256]{2,1,0:T(8,128)(2,1)S(1)}, bf16[2,128,256]{2,1,0:T(8,128)(2,1)S(1)}, u32[]{:S(2)}, u32[]{:S(2)}) collective-permute-start(bf16[2,128,256]{2,1,0:T(8,128)(2,1)S(1)} %get-tuple-element.243), channel_id=1, source_target_pairs={{4,0},{8,4},{12,8},{16,12},{20,16},{24,20},{28,24},{5,1},{9,5},{13... | collective-permute-start | bytes 393224 | tf_op jit(solution)/shard_map/ppermute | solution.py:18
  296.3 1.0 copy-start.5
  297.4 0.9 copy-start.6
  360.7 24.2 %copy-start.4 = (bf16[4,128,16,128]{3,2,1,0:T(8,128)(2,1)S(1)}, bf16[4,128,16,128]{3,2,1,0:T(8,128)(2,1)}, u32[]{:S(2)}) copy-start(bf16[4,128,16,128]{3,2,1,0:T(8,128)(2,1)} %get-tuple-element.93) | copy-start | bytes 6291460
  361.7 12.8 %all-to-all-start.8 = ((bf16[512,2,128]{2,1,0:T(2,128)(2,1)}), bf16[512,2,128]{2,1,0:T(2,128)(2,1)S(1)}, u32[]{:S(2)}, u32[]{:S(2)}) async-start(bf16[512,2,128]{2,1,0:T(2,128)(2,1)} %reshape_squeeze.7), calls=%async_computation.8 | async-start | bytes 524288 | tf_op jit(solution)/shard_map/all_to_all | solution.py:232
  435.3 50.9 %all-to-all-start.4 = ((bf16[512,16,128]{2,1,0:T(8,128)(2,1)}), bf16[512,16,128]{2,1,0:T(8,128)(2,1)S(1)}, u32[]{:S(2)}, u32[]{:S(2)}) async-start(bf16[512,16,128]{2,1,0:T(8,128)(2,1)} %bitcast.277), calls=%async_computation.4 | async-start | bytes 4194304 | tf_op jit(solution)/shard_map/all_to_all | solution.py:229
  438.9 1.9 copy-start
Sparse Core Ops, SparseCore 0:
  35.9 36.1 all-gather.1
  103.1 58.3 all-reduce.8
  295.1 58.1 all-reduce.6
where the time goes:
time: 497 us; the launch traced here: 495 us
  waiting for transfers between devices  204 us (41%)
  local copies, waits for them, and re-layouts  85.5 us (17%)
  blocking collectives  60.8 us (12%)
  matrix products  46.3 us (9%)
  other arithmetic  39.6 us (8%)
  starting transfers between devices  36.1 us (7%)
  between operations  19.4 us (4%)
    psum x1, waiting for transfers between devices, per_device(): lax.psum(global_terms.astype(jnp.bfloat16), 'seq').astype(jnp.float32)  50.8 us
    all_to_all x1, blocking collectives, per_device(): lax.all_to_all(query_grad_all, 'head', split_axis=0, concat_axis=1, tiled...  50.3 us
    psum x1, waiting for transfers between devices, from_root(): return lax.psum(block, axis)  47.8 us
    all_to_all x1, waiting for transfers between devices, per_device(): lax.all_to_all(out_all, 'head', split_axis=0, concat_axis=1, tiled=True)  43.4 us
    all_to_all x1, waiting for transfers between devices, per_device(): lax.all_to_all(output_gradient, 'head', split_axis=1, concat_axis=0, tile...  37.3 us
    unnamed x42, local copies, waits for them, and re-layouts  13.2 us
    dot_general x4, matrix products, attend(): jnp.einsum('qkgd,tbkd->kgqtb', grad_grid, value_t, preferred_element_type...  13 us
    dynamic_update_slice x12, local copies, waits for them, and re-layouts, per_device(): lax.scan(attend, 0, (query_loc.reshape(blocks, BLOCK_TOKENS, heads_q, hea...  12.2 us
  transfers between devices with their start and end apart: 14, of which 8 were waited for; matrix products, arithmetic and copies ran while one was open for 9% of the time, Pallas kernels for 0%

commit v1 on v0

--- a/solution.py
+++ b/solution.py
@@ -22,7 +22,7 @@
 
 def from_root(block, axis, owner):
     block = jnp.where(lax.axis_index(axis) == owner, block, jnp.zeros_like(block))
-    return lax.psum(block, axis)
+    return jnp.sum(jax.lax.all_gather(block, axis), 0)
 
 
 def per_device(queries, keys, values, output_gradient, global_blocks, random_blocks):

time: 497 us -> 474 us (0.954)
  waiting for transfers between devices: 204 us -> 179 us
    psum x1 -> x0, waiting for transfers between devices: 47.8 us -> none  [from_root(): return lax.psum(block, axis)]
    all_to_all x1, waiting for transfers between devices: 0.01 us -> 15.9 us  [per_device(): lax.all_to_all(queries, 'head', split_axis=1, concat_axis=0, tiled=True)]
    all_gather x1, waiting for transfers between devices: 0.01 us -> 12.3 us  [per_device(): everything = lax.all_gather(kv_pair, 'seq', axis=1, tiled=True)]
    unnamed x42 -> x40, local copies, waits for them, and re-layouts: 13.2 us -> 15.3 us
  transfers between devices with their start and end apart: 14 -> 15, of which waited for: 8 -> 9; matrix products, arithmetic and copies ran while one was open for 9% -> 10% of each run, Pallas kernels for 0% -> 0%
where the time goes in v1:
time: 474 us; the launch traced here: 471 us
  waiting for transfers between devices  179 us (38%)
  local copies, waits for them, and re-layouts  86.9 us (18%)
  blocking collectives  60.8 us (13%)
  matrix products  46.3 us (10%)
  other arithmetic  39.3 us (8%)
  starting transfers between devices  36.3 us (8%)
  between operations  19.4 us (4%)
    all_to_all x1, blocking collectives, per_device(): lax.all_to_all(query_grad_all, 'head', split_axis=0, concat_axis=1, tiled...  50.3 us
    psum x1, waiting for transfers between devices, per_device(): lax.psum(global_terms.astype(jnp.bfloat16), 'seq').astype(jnp.float32)  49 us
    all_to_all x1, waiting for transfers between devices, per_device(): lax.all_to_all(out_all, 'head', split_axis=0, concat_axis=1, tiled=True)  43.4 us
    all_to_all x1, waiting for transfers between devices, per_device(): lax.all_to_all(output_gradient, 'head', split_axis=1, concat_axis=0, tile...  41.1 us
    all_to_all x1, waiting for transfers between devices, per_device(): lax.all_to_all(queries, 'head', split_axis=1, concat_axis=0, tiled=True)  15.9 us
    unnamed x40, local copies, waits for them, and re-layouts  15.3 us
    dot_general x4, matrix products, attend(): jnp.einsum('qkgd,tbkd->kgqtb', grad_grid, value_t, preferred_element_type...  13 us
    all_gather x1, waiting for transfers between devices, per_device(): everything = lax.all_gather(kv_pair, 'seq', axis=1, tiled=True)  12.3 us
  transfers between devices with their start and end apart: 15, of which 9 were waited for; matrix products, arithmetic and copies ran while one was open for 10% of the time, Pallas kernels for 0%

profile of v1, /device:TPU:0, one launch (start us, length us, event | category | flops | bytes accessed | tf_op | source)
XLA Modules:
  0.0 471.3 jit_solution(17904135037849792967)
XLA Ops:
  8.9 6.3 %all-to-all-start = ((bf16[128,8,128]{2,0,1:T(8,128)(2,1)}), bf16[128,8,128]{2,0,1:T(8,128)(2,1)S(1)}, u32[]{:S(2)}, u32[]{:S(2)}) async-start(bf16[128,8,128]{2,0,1:T(8,128)(2,1)} %copy.306), calls=%async_computation | async-start | bytes 524288 | tf_op jit(solution)/shard_map/all_to_all | solution.py:31
  21.3 2.8 all-to-all-done
  24.1 3.4 all-to-all-start.1
  31.8 2.7 all-to-all-done.1
  37.8 4.3 copy.315
  42.1 3.6 all-to-all-start.3
  45.7 4.3 copy.314
  50.0 41.1 %all-to-all-done.3 = bf16[128,64,128]{2,0,1:T(8,128)(2,1)S(1)} async-done(((bf16[128,64,128]{2,0,1:T(8,128)(2,1)}), bf16[128,64,128]{2,0,1:T(8,128)(2,1)S(1)}, u32[]{:S(2)}, u32[]{:S(2)}) %all-to-all-start.3) | async-done | bytes 2097184 | tf_op jit(solution)/shard_map/all_to_all | solution.py:33
  91.1 4.5 all-to-all-start.2
  101.6 3.1 collective-permute-done.1
  108.4 2.6 copy.316
  111.0 12.3 %all-gather.6.cloned.1.call-done = bf16[2,4096,256]{2,1,0:T(8,128)(2,1)} async-done(((bf16[2,512,256]{2,1,0:T(8,128)(2,1)}), bf16[2,4096,256]{2,1,0:T(8,128)(2,1)}) %all-gather.6.cloned.1.call-update) | async-done | bytes 4194320 | tf_op jit(solution)/shard_map/all_gather | solution.py:88
  123.3 2.8 gather_fusion
  127.5 15.9 %all-to-all-done.2 = bf16[128,64,128]{2,0,1:T(8,128)(2,1)} async-done(((bf16[128,64,128]{2,0,1:T(8,128)(2,1)}), bf16[128,64,128]{2,0,1:T(8,128)(2,1)}, u32[]{:S(2)}, u32[]{:S(2)}) %all-to-all-start.2) | async-done | bytes 2097184 | tf_op jit(solution)/shard_map/all_to_all | solution.py:30
  143.4 101.8 %while.16 = (s32[]{:T(128)}, bf16[4,128,16,128]{3,2,1,0:T(8,128)(2,1)}, bf16[4,128,16,128]{3,2,1,0:T(8,128)(2,1)}, f32[4,8,2,128,256]{3,4,1,2,0:T(8,128)}, s32[4...) while((s32[]{:T(128)}, ...), condition=%wide.region_7.8_spmd, body=%wide.region_3.7_spmd.sunk | while | flops 3265259520 | bytes 89202968 | solution.py:170
  149.7 1.9 bitcast_reduce_fusion.4
  151.7 1.7 fusion.113
  153.4 2.2 fusion.114
  158.7 3.2 fusion.115
  175.1 1.9 bitcast_reduce_fusion.4
  178.8 2.2 fusion.114
  184.2 3.2 fusion.115
  200.6 1.9 bitcast_reduce_fusion.4
  204.2 2.2 fusion.114
  209.6 3.2 fusion.115
  226.0 1.9 bitcast_reduce_fusion.4
  229.7 2.2 fusion.114
  235.0 3.2 fusion.115
  245.2 9.1 %copy.322 = f32[4,8,2,128,256]{4,3,2,0,1:T(8,128)} copy(f32[4,8,2,128,256]{3,4,1,2,0:T(8,128)} %get-tuple-element.94) | data formatting | bytes 16777216 | tf_op jit(solution)/shard_map/while | solution.py:170
  254.4 2.1 slice.167
  257.5 2.0 copy.338
  259.6 3.7 all-to-all-start.6
  263.6 2.2 slice_bitcast_fusion.2
  267.3 2.4 collective-permute-start.2
  271.0 2.5 slice_reduce_fusion
  277.2 3.8 scatter-add.9
  281.0 49.0 %all-reduce.5.cloned.1.call-done = bf16[2,2,128,256]{2,3,0,1:T(8,128)(2,1)} async-done(((bf16[2,2,128,256]{2,3,0,1:T(8,128)(2,1)}), bf16[2,2,128,256]{2,3,0,1:T(8,128)(2,1)}) %all-reduce.5.cloned.1.call-update) | async-done | bytes 262160 | tf_op jit(solution)/shard_map/psum | solution.py:201
  329.9 1.9 copy.327
  331.8 2.4 multiply_reduce_fusion.1
  334.2 3.1 fusion.50
  338.4 4.6 all-to-all-start.8
  343.1 8.1 %all-to-all-done.8 = bf16[512,2,128]{2,1,0:T(2,128)(2,1)S(1)} async-done(((bf16[512,2,128]{2,1,0:T(2,128)(2,1)}), bf16[512,2,128]{2,1,0:T(2,128)(2,1)S(1)}, u32[]{:S(2)}, u32[]{:S(2)}) %all-to-all-start.8) | async-done | bytes 262176 | tf_op jit(solution)/shard_map/all_to_all | solution.py:232
  351.1 10.4 %all_to_all.137 = bf16[512,2,128]{2,1,0:T(2,128)(2,1)S(1)} all-to-all(bf16[512,2,128]{2,1,0:T(2,128)(2,1)S(1)} %reshape_squeeze.6), channel_id=1, replica_groups=mesh['seq'=8,'head'=4] {'head'}, dimensions={0} | all-to-all | bytes 524288 | tf_op jit(solution)/shard_map/all_to_all | solution.py:231
  361.6 50.3 %all_to_all.138 = bf16[512,16,128]{2,1,0:T(8,128)(2,1)} all-to-all(bf16[512,16,128]{2,1,0:T(8,128)(2,1)S(1)} %bitcast.280), channel_id=1, replica_groups=mesh['seq'=8,'head'=4] {'head'}, dimensions={0} | all-to-all | bytes 4194304 | tf_op jit(solution)/shard_map/all_to_all | solution.py:230
  411.9 3.6 all-to-all-start.4
  417.4 2.0 copy.321
  419.4 43.4 %all-to-all-done.4 = bf16[512,16,128]{2,1,0:T(8,128)(2,1)S(1)} async-done(((bf16[512,16,128]{2,1,0:T(8,128)(2,1)}), bf16[512,16,128]{2,1,0:T(8,128)(2,1)S(1)}, u32[]{:S(2)}, u32[]{:S(2)}) %all-to-all-start.4) | async-done | bytes 2097184 | tf_op jit(solution)/shard_map/all_to_all | solution.py:229
  462.8 2.0 copy.319
  (204 shorter events, 99.1 us)
Async XLA Ops:
  7.2 20.4 %copy-start.13 = (s32[2]{0:T(128)S(1)}, s32[2]{0:T(128)}, u32[]{:S(2)}) copy-start(s32[2]{0:T(128)} %param.16) | copy-start | bytes 28
  8.9 15.3 %all-to-all-start = ((bf16[128,8,128]{2,0,1:T(8,128)(2,1)}), bf16[128,8,128]{2,0,1:T(8,128)(2,1)S(1)}, u32[]{:S(2)}, u32[]{:S(2)}) async-start(bf16[128,8,128]{2,0,1:T(8,128)(2,1)} %copy.306), calls=%async_computation | async-start | bytes 524288 | tf_op jit(solution)/shard_map/all_to_all | solution.py:31
  15.9 0.5 copy-start.8
  24.1 10.4 %all-to-all-start.1 = ((bf16[128,8,128]{2,0,1:T(8,128)(2,1)}), bf16[128,8,128]{2,0,1:T(8,128)(2,1)S(1)}, u32[]{:S(2)}, u32[]{:S(2)}) async-start(bf16[128,8,128]{2,0,1:T(8,128)(2,1)} %copy.308), calls=%async_computation.1 | async-start | bytes 524288 | tf_op jit(solution)/shard_map/all_to_all | solution.py:32
  27.5 78.1 %all-gather.10.cloned.1.call-start = ((), (), s32[]{:S(2)}) async-start(), calls=%async_computation.12 | async-start | bytes 1179648 | tf_op jit(solution)/shard_map/all_gather | solution.py:25
  35.8 71.2 %all-gather.8.cloned.1.call-start = ((), (), s32[]{:S(2)}) async-start(), calls=%async_computation.11 | async-start | bytes 1179648 | tf_op jit(solution)/shard_map/all_gather | solution.py:25
  36.5 86.8 %all-gather.6.cloned.1.call-start = ((), (), s32[]{:S(2)}) async-start(), calls=%async_computation.9 | async-start | bytes 4718592 | tf_op jit(solution)/shard_map/all_gather | solution.py:88
  37.0 0.8 copy-start.1
  42.1 49.0 %all-to-all-start.3 = ((bf16[128,64,128]{2,0,1:T(8,128)(2,1)}), bf16[128,64,128]{2,0,1:T(8,128)(2,1)S(1)}, u32[]{:S(2)}, u32[]{:S(2)}) async-start(bf16[128,64,128]{2,0,1:T(8,128)(2,1)} %copy.315), calls=%async_computation.3 | async-start | bytes 4194304 | tf_op jit(solution)/shard_map/all_to_all | solution.py:33
  50.0 45.7 %copy-start.12 = (s32[32,3]{0,1:T(4,128)S(1)}, s32[32,3]{0,1:T(4,128)}, u32[]{:S(2)}) copy-start(s32[32,3]{0,1:T(4,128)} %param.17) | copy-start | bytes 1156
  50.0 48.4 %copy-start.2 = (bf16[2,512,256]{2,1,0:T(8,128)(2,1)S(1)}, bf16[2,512,256]{2,1,0:T(8,128)(2,1)}, u32[]{:S(2)}) copy-start(bf16[2,512,256]{2,1,0:T(8,128)(2,1)} %copy-done.1) | copy-start | bytes 1572868
  91.1 52.3 %all-to-all-start.2 = ((bf16[128,64,128]{2,0,1:T(8,128)(2,1)}), bf16[128,64,128]{2,0,1:T(8,128)(2,1)}, u32[]{:S(2)}, u32[]{:S(2)}) async-start(bf16[128,64,128]{2,0,1:T(8,128)(2,1)} %copy.314), calls=%async_computation.2 | async-start | bytes 4194304 | tf_op jit(solution)/shard_map/all_to_all | solution.py:30
  97.4 8.2 %copy-start.6 = (s32[8,12]{1,0:T(8,128)}, s32[8,12]{1,0:T(8,128)S(1)}, u32[]{:S(2)}) copy-start(s32[8,12]{1,0:T(8,128)S(1)} %copy.334) | copy-start | bytes 1156
  98.4 3.2 collective-permute-start
  99.7 5.0 %collective-permute-start.1 = (bf16[2,128,256]{2,1,0:T(8,128)(2,1)S(1)}, bf16[2,128,256]{2,1,0:T(8,128)(2,1)S(1)}, u32[]{:S(2)}, u32[]{:S(2)}) collective-permute-start(bf16[2,128,256]{2,1,0:T(8,128)(2,1)S(1)} %get-tuple-element.247), channel_id=1, source_target_pairs={{4,0},{8,4},{12,8},{16,12},{20,16},{24,20},{28,24},{5,1},{9,5},{13... | collective-permute-start | bytes 393224 | tf_op jit(solution)/shard_map/ppermute | solution.py:18
  254.4 2.1 copy-start.11
  259.6 3.8 copy-start.9
  259.6 3.8 copy-start.14
  259.6 3.9 copy-start.7
  259.6 3.9 copy-start.10
  259.6 3.9 copy-start.15
  259.6 74.6 %all-to-all-start.6 = ((bf16[16,2,128,256]{3,2,1,0:T(8,128)(2,1)}), bf16[16,2,128,256]{3,2,1,0:T(8,128)(2,1)S(1)}, u32[]{:S(2)}, u32[]{:S(2)}) async-start(bf16[16,2,128,256]{3,2,1,0:T(8,128)(2,1)} %copy.338), calls=%async_computation.6 | async-start | bytes 4194304 | tf_op jit(solution)/shard_map/all_to_all | solution.py:216
  263.3 66.6 %all-reduce.5.cloned.1.call-start = ((), (), s32[]{:S(2)}) async-start(), calls=%async_computation.10 | async-start | bytes 524288 | tf_op jit(solution)/shard_map/psum | solution.py:201
  267.3 7.5 %collective-permute-start.2 = (bf16[2,128,256]{2,1,0:T(8,128)(2,1)S(1)}, bf16[2,128,256]{2,1,0:T(8,128)(2,1)S(1)}, u32[]{:S(2)}, u32[]{:S(2)}) collective-permute-start(bf16[2,128,256]{2,1,0:T(8,128)(2,1)S(1)} %get-tuple-element.240), channel_id=1, source_target_pairs={{0,4},{4,8},{8,12},{12,16},{16,20},{20,24},{24,28},{1,5},{5,9},{9,... | collective-permute-start | bytes 393224 | tf_op jit(solution)/shard_map/ppermute | solution.py:17
  269.7 5.2 %collective-permute-start.3 = (bf16[2,128,256]{2,1,0:T(8,128)(2,1)S(1)}, bf16[2,128,256]{2,1,0:T(8,128)(2,1)S(1)}, u32[]{:S(2)}, u32[]{:S(2)}) collective-permute-start(bf16[2,128,256]{2,1,0:T(8,128)(2,1)S(1)} %get-tuple-element.241), channel_id=1, source_target_pairs={{4,0},{8,4},{12,8},{16,12},{20,16},{24,20},{28,24},{5,1},{9,5},{13... | collective-permute-start | bytes 393224 | tf_op jit(solution)/shard_map/ppermute | solution.py:18
  274.8 1.0 copy-start.4
  275.9 0.9 copy-start.5
  337.4 24.2 %copy-start.3 = (bf16[4,128,16,128]{3,2,1,0:T(8,128)(2,1)S(1)}, bf16[4,128,16,128]{3,2,1,0:T(8,128)(2,1)}, u32[]{:S(2)}) copy-start(bf16[4,128,16,128]{3,2,1,0:T(8,128)(2,1)} %get-tuple-element.93) | copy-start | bytes 6291460
  338.4 12.8 %all-to-all-start.8 = ((bf16[512,2,128]{2,1,0:T(2,128)(2,1)}), bf16[512,2,128]{2,1,0:T(2,128)(2,1)S(1)}, u32[]{:S(2)}, u32[]{:S(2)}) async-start(bf16[512,2,128]{2,1,0:T(2,128)(2,1)} %reshape_squeeze.7), calls=%async_computation.8 | async-start | bytes 524288 | tf_op jit(solution)/shard_map/all_to_all | solution.py:232
  411.9 50.9 %all-to-all-start.4 = ((bf16[512,16,128]{2,1,0:T(8,128)(2,1)}), bf16[512,16,128]{2,1,0:T(8,128)(2,1)S(1)}, u32[]{:S(2)}, u32[]{:S(2)}) async-start(bf16[512,16,128]{2,1,0:T(8,128)(2,1)} %bitcast.281), calls=%async_computation.4 | async-start | bytes 4194304 | tf_op jit(solution)/shard_map/all_to_all | solution.py:229
  415.5 1.9 copy-start
Sparse Core Ops, SparseCore 0:
  35.9 22.9 all-gather.9
  61.4 23.3 all-gather.7
  86.7 36.5 all-gather.5
  273.6 56.2 all-reduce.4
